TPU v7x, 512 devices: a whole 4x4x16 slice. The times are simulated.
512 devices in a mesh: seq: 128 (over x, z, core), head: 4 (over y).
Axes of the slice: x: 4, y: 4, z: 16, core: 2. Of those that a mesh axis runs over, the one named last changes fastest.
Arguments:
- hidden: bfloat16 [32768, 2560], P(('seq', 'head')), may hold values from -6 to 6
- w_values: bfloat16 [2560, 2560], P('seq', 'head'), may hold values from -0.125 to 0.125
- w_gates: bfloat16 [2560, 2560], P('seq', 'head'), may hold values from -0.125 to 0.125
- w_steps: bfloat16 [2560, 40], P('seq', 'head'), may hold values from -0.0625 to 0.0625
- w_states: bfloat16 [2560, 256], P('seq'), may hold values from -0.125 to 0.125
- conv_weight: float32 [4, 2816], replicated, may hold values from -3 to 3
- conv_bias: float32 [2816], replicated, may hold values from -3 to 3
- step_bias: float32 [40], P('head'), may hold values from -1 to 0.5
- decay_rate: float32 [40], P('head'), may hold values from 0 to 1, as said below
- skip_gain: float32 [40], P('head'), may hold values from 1 to 8
- norm_gain: float32 [2560], replicated, may hold values from 0.5 to 1.5
- lengths: int32 [64], replicated, may hold values from 256 to 768, as said below
Outputs:
- gated_out: bfloat16 [32768, 2560], P(('seq', 'head'))
- final_states: float32 [128, 40, 64, 128], P('seq', 'head')
Inputs may be any that keep to these rules, and one draw needn't show every extreme that they name: Prompts are packed in order, each holding 256 to 768 tokens; the lengths sum to 32768. `decay_rate`: positive rates.
All inputs are finite; a program needn't handle non-finite values.
Results may differ from a plain program's by a relative error of at most 0.01.
Values may be sent and summed in bfloat16 or wider, within the bound.
No kernel may reach another device: no remote copies, remote signals or barrier semaphores. Data moves between devices by JAX's collectives and lax.ppermute only.
A program may use at most 128 MiB of HBM per device.

v0:
```python
import jax
import jax.numpy as jnp
from jax import lax
from jax.sharding import Mesh, PartitionSpec as P

STRETCH = 256
SEQ = ("x", "z", "c")
epsilon = 1e-05


def from_behind(block, axis, distance):
    devices = range(lax.psum(1, axis))
    route = [(i - distance, i) for i in devices if i - distance in devices]
    return lax.ppermute(block, axis, route)


def segments_at(positions, prompt_ends):
    counted = jnp.sum((prompt_ends[None, :] <= positions[:, None]).astype(jnp.int32), axis=1)
    return jnp.where(positions < 0, -1, counted)


def on_device(
    hidden,
    w_values,
    w_gates,
    w_steps,
    w_states,
    conv_weight,
    conv_bias,
    step_bias,
    decay_rate,
    skip_gain,
    norm_gain,
    lengths,
):
    groups = lax.axis_size("head")
    group_index = lax.axis_index("head")
    block_index = lax.axis_index(SEQ)
    local_width = w_values.shape[1]
    inner_width = local_width * groups
    local_heads = decay_rate.shape[0]
    head_width = local_width // local_heads
    state_width = w_states.shape[1] // 2
    conv_taps = conv_weight.shape[0]
    prompt_ends = jnp.cumsum(lengths)
    block_hidden = lax.all_to_all(
        jnp.broadcast_to(hidden[None], (groups,) + hidden.shape), "head", 0, 0, tiled=True
    ).reshape(groups * hidden.shape[0], hidden.shape[1])
    block_rows = block_hidden.shape[0]
    sub_rows = block_rows // groups
    step_width = w_steps.shape[1]
    merged = jnp.concatenate([w_values, w_states, w_gates, w_steps], axis=1)
    shard_rows = merged.shape[0]
    padded_rows = -(-shard_rows // 16) * 16
    half = local_width + 2 * state_width
    merged = jnp.pad(merged, ((0, padded_rows - shard_rows), (0, 2 * half - merged.shape[1])))
    halves = jnp.stack([merged[:, :half], merged[:, half:]])
    own_half = lax.all_to_all(halves, "c", 0, 0, tiled=True).reshape(2 * padded_rows, half)
    own_half = lax.all_gather(own_half, "x", axis=0, tiled=True)
    early_start = block_index * block_rows
    ext_positions = (
        early_start - (conv_taps - 1) + jnp.arange(block_rows + conv_taps - 1, dtype=jnp.int32)
    )
    positions = early_start + jnp.arange(block_rows, dtype=jnp.int32)
    early_ids = (
        segments_at(ext_positions, prompt_ends),
        segments_at(positions, prompt_ends),
        segments_at(positions + 1, prompt_ends),
        segments_at(positions - 1, prompt_ends),
    )
    block_hidden, own_half, early_ids = lax.optimization_barrier(
        (block_hidden, own_half, early_ids)
    )
    ext_ids, segment_ids, next_ids, before_ids = early_ids
    own_half = lax.all_gather(own_half, "z", axis=0, tiled=True)
    other_half = lax.ppermute(own_half, "c", [(0, 1), (1, 0)])
    x_size = lax.psum(1, "x")
    z_size = lax.psum(1, "z")
    c_size = lax.psum(1, "c")
    core_index = lax.axis_index("c")

    def spread_rows(rows):
        count = rows.shape[0]
        split = rows.reshape(count, x_size, z_size, c_size, shard_rows)
        split = jnp.pad(split, ((0, 0), (0, 0), (0, 0), (0, 0), (0, padded_rows - shard_rows)))
        split = jnp.transpose(split, (0, 2, 1, 3, 4))
        return split.reshape(count, x_size * z_size * c_size * padded_rows)

    rim_hidden = from_behind(block_hidden[block_rows - (conv_taps - 1) :], SEQ, 1)
    rim_count = rim_hidden.shape[0]
    both_rows = jnp.concatenate(
        [block_hidden, rim_hidden, jnp.zeros((8 - rim_count, block_hidden.shape[1]), jnp.bfloat16)]
    )
    spread = spread_rows(both_rows)
    with_own = jnp.dot(spread, own_half, preferred_element_type=jnp.float32)
    with_other = jnp.dot(spread, other_half, preferred_element_type=jnp.float32)
    first_cols = jnp.where(core_index == 0, with_own, with_other)
    second_cols = jnp.where(core_index == 0, with_other, with_own)
    projected = jnp.concatenate([first_cols, second_cols], axis=1)
    conv_end = local_width + 2 * state_width
    prior_rim = projected[block_rows : block_rows + rim_count, :conv_end].astype(jnp.bfloat16)
    projected = projected[:block_rows]
    pre_rows = projected[:, :conv_end].astype(jnp.bfloat16)
    gates_sum = projected[:, conv_end : conv_end + local_width]
    steps_sum = projected[:, conv_end + local_width : conv_end + local_width + step_width]
    head_gates = gates_sum.astype(jnp.bfloat16)
    gates_tokens = lax.all_to_all(
        head_gates.reshape(groups, sub_rows, local_width), "head", 0, 2, tiled=True
    ).reshape(sub_rows, inner_width)
    local_taps = jnp.concatenate(
        [
            lax.dynamic_slice_in_dim(conv_weight, group_index * local_width, local_width, 1),
            conv_weight[:, inner_width:],
        ],
        axis=1,
    )
    local_bias = jnp.concatenate(
        [
            lax.dynamic_slice_in_dim(conv_bias, group_index * local_width, local_width, 0),
            conv_bias[inner_width:],
        ],
        axis=0,
    )
    block_start = block_index * block_rows
    extended = jnp.concatenate([prior_rim, pre_rows], axis=0)
    own_ids = ext_ids[conv_taps - 1 :]
    filtered = jnp.zeros(pre_rows.shape, jnp.float32) + local_bias[None, :]
    for offset in range(conv_taps):
        matches = (ext_ids[offset : offset + block_rows] == own_ids).astype(jnp.float32)
        filtered = (
            filtered
            + local_taps[offset][None, :]
            * extended[offset : offset + block_rows].astype(jnp.float32)
            * matches[:, None]
        )
    conv_out = jax.nn.silu(filtered).astype(jnp.bfloat16)
    head_values = conv_out[:, :local_width]
    both_states = conv_out[:, local_width:]
    stretch_rows = STRETCH
    stretches = block_rows // stretch_rows
    stretch_ids = segment_ids.reshape(stretches, stretch_rows)
    prior_ids = before_ids.reshape(stretches, stretch_rows)[:, 0]
    ends_mask = (segment_ids != next_ids).reshape(stretches, stretch_rows)
    step_sizes = jax.nn.softplus(steps_sum + step_bias[None, :])
    decay_steps = step_sizes * decay_rate[None, :]
    log_decay = -jnp.cumsum(decay_steps.reshape(stretches, stretch_rows, local_heads), axis=1)
    decay_heads = jnp.swapaxes(log_decay, 1, 2)
    step_heads = jnp.swapaxes(step_sizes.reshape(stretches, stretch_rows, local_heads), 1, 2)
    values = head_values.reshape(stretches, stretch_rows, local_heads, head_width)
    write_state = both_states[:, :state_width].reshape(stretches, stretch_rows, state_width)
    read_state = both_states[:, state_width:].reshape(stretches, stretch_rows, state_width)
    intersection = jnp.einsum(
        "ctn,csn->cts", read_state, write_state, preferred_element_type=jnp.float32
    )
    token_order = jnp.arange(stretch_rows, dtype=jnp.int32)
    causal = token_order[:, None] >= token_order[None, :]
    allowed = causal[None] & (stretch_ids[:, :, None] == stretch_ids[:, None, :])
    spread = decay_heads[:, :, :, None] - decay_heads[:, :, None, :]
    weights = (
        jnp.where(allowed[:, None], jnp.exp(jnp.minimum(spread, 0.0)), 0.0)
        * step_heads[:, :, None, :]
    )
    scores = (intersection[:, None] * weights).astype(jnp.bfloat16)
    within_stretch = jnp.einsum(
        "chts,cshp->cthp", scores, values, preferred_element_type=jnp.float32
    )
    last_ids = stretch_ids[:, -1]
    tail_decay = decay_heads[:, :, -1:]
    keep_tail = (stretch_ids == last_ids[:, None])[:, None, :]
    tail_coef = (
        jnp.where(keep_tail, jnp.exp(jnp.minimum(tail_decay - decay_heads, 0.0)), 0.0) * step_heads
    )
    tail_rows = (values.astype(jnp.float32) * jnp.swapaxes(tail_coef, 1, 2)[:, :, :, None]).astype(
        jnp.bfloat16
    )
    stretch_states = jnp.einsum(
        "clhp,cln->chpn", tail_rows, write_state, preferred_element_type=jnp.float32
    )
    stretch_gates = (
        jnp.exp(decay_heads[:, :, -1]) * (last_ids == prior_ids).astype(jnp.float32)[:, None]
    )
    own_gate = jnp.broadcast_to(stretch_gates[0][:, None, None], (local_heads, 8, state_width))
    packed = jnp.concatenate([stretch_states[0], own_gate], axis=1).astype(jnp.bfloat16)
    p1 = from_behind(packed, SEQ, 1)
    p2 = from_behind(packed, SEQ, 2)
    p3 = from_behind(packed, SEQ, 3)
    g1 = p1[:, head_width : head_width + 1, :1]
    g2 = p2[:, head_width : head_width + 1, :1]
    p1, p2, p3, g1, g2 = (part.astype(jnp.float32) for part in (p1, p2, p3, g1, g2))
    incoming = p1[:, :head_width] + g1 * (p2[:, :head_width] + g2 * p3[:, :head_width])
    arriving = incoming[None]
    carry_mask = (stretch_ids == prior_ids[:, None]).astype(jnp.float32)
    carry_decay = jnp.exp(log_decay) * carry_mask[:, :, None]
    from_before = (
        jnp.einsum(
            "cln,chpn->clhp",
            read_state,
            arriving.astype(jnp.bfloat16),
            preferred_element_type=jnp.float32,
        )
        * carry_decay[:, :, :, None]
    )
    result = (
        within_stretch + from_before + skip_gain[None, None, :, None] * values.astype(jnp.float32)
    )
    ssm_rows = result.reshape(block_rows, local_width).astype(jnp.bfloat16)
    end_weight = ends_mask.astype(jnp.float32)
    has_end = jnp.sum(end_weight, axis=1)
    end_decay = jnp.sum(decay_heads * end_weight[:, None, :], axis=2)
    end_ids = jnp.sum(jnp.where(ends_mask, stretch_ids, 0), axis=1)
    keep_end = ((stretch_ids == end_ids[:, None]) & (has_end[:, None] > 0))[:, None, :]
    end_coef = (
        jnp.where(keep_end, jnp.exp(jnp.minimum(end_decay[:, :, None] - decay_heads, 0.0)), 0.0)
        * step_heads
    )
    end_rows = (values.astype(jnp.float32) * jnp.swapaxes(end_coef, 1, 2)[:, :, :, None]).astype(
        jnp.bfloat16
    )
    end_states = jnp.einsum(
        "clhp,cln->chpn", end_rows, write_state, preferred_element_type=jnp.float32
    )
    end_carry = (
        jnp.exp(end_decay) * ((end_ids == prior_ids) & (has_end > 0)).astype(jnp.float32)[:, None]
    )
    end_states = end_states + end_carry[:, :, None, None] * arriving
    final_block = jnp.sum(end_states, axis=0)[None]
    y_tokens = lax.all_to_all(
        ssm_rows.reshape(groups, sub_rows, local_width), "head", 0, 2, tiled=True
    ).reshape(sub_rows, inner_width)
    token_rows = (y_tokens.astype(jnp.float32), gates_tokens.astype(jnp.float32))
    gated = token_rows[0] * jax.nn.silu(token_rows[1])
    mean_square = jnp.mean(gated * gated, axis=1)
    scaled = gated * lax.rsqrt(mean_square + epsilon)[:, None] * norm_gain[None, :]
    gated_out = scaled.astype(jnp.bfloat16)
    return (gated_out, final_block)


def solution(mesh):
    seq_size, head_size = mesh.devices.shape
    fine = Mesh(mesh.devices.reshape(4, seq_size // 8, 2, head_size), SEQ + ("head",))
    in_specs = (
        P(SEQ + ("head",), None),
        P(SEQ, "head"),
        P(SEQ, "head"),
        P(SEQ, "head"),
        P(SEQ, None),
        P(),
        P(),
        P("head"),
        P("head"),
        P("head"),
        P(),
        P(),
    )
    out_specs = (P(SEQ + ("head",), None), P(SEQ, "head", None, None))
    return jax.shard_map(
        on_device, mesh=fine, in_specs=in_specs, out_specs=out_specs, check_vma=False
    )
```

profile of v0, /device:TPU:1, one launch (start us, length us, event | category | flops | bytes accessed | tf_op | source)
XLA Modules:
  0.0 220.1 jit_solution(13898539905793476150)
XLA Ops:
  7.2 0.8 copy.129
  8.0 0.8 fusion.32
  8.8 0.7 pad_maximum_fusion.2
  9.4 10.2 %all-to-all-start.1 = ((bf16[2,32,896]{2,1,0:T(8,128)(2,1)}), bf16[2,32,896]{2,1,0:T(8,128)(2,1)S(1)}, u32[]{:S(2)}, u32[]{:S(2)}) async-start(bf16[2,32,896]{2,1,0:T(8,128)(2,1)} %pad_maximum_fusion.2), calls=%async_computation.1 | async-start | bytes 229376 | tf_op jit(solution)/shard_map/all_to_all | solution.py:58
  19.7 0.7 copy.130
  20.4 0.1 reduce-window.18
  20.5 0.1 reduce.8
  20.6 0.1 convert_reduce_fusion
  20.8 2.1 broadcast_in_dim.39
  22.9 3.5 %all-to-all-start = ((bf16[4,64,2560]{2,1,0:T(8,128)(2,1)}), bf16[4,64,2560]{2,1,0:T(8,128)(2,1)S(1)}, u32[]{:S(2)}, u32[]{:S(2)}) async-start(bf16[4,64,2560]{2,1,0:T(8,128)(2,1)} %broadcast_in_dim.39), calls=%async_computation | async-start | bytes 2621440 | tf_op jit(solution)/shard_map/all_to_all | solution.py:46
  26.5 0.1 convert_reduce_fusion.1
  26.6 11.1 %all_gather.6 = bf16[256,896]{1,0:T(8,128)(2,1)} all-gather(bf16[64,896]{1,0:T(8,128)(2,1)S(1)} %bitcast.148), channel_id=1, replica_groups=mesh['x'=4,'z'=16,'c'=2,'head'=4] {'x'}, dimensions={0}, use_global_device_ids=true | all-gather | bytes 573440 | tf_op jit(solution)/shard_map/all_gather | solution.py:59
  37.7 6.4 %all-to-all-done = bf16[4,64,2560]{2,1,0:T(8,128)(2,1)S(1)} async-done(((bf16[4,64,2560]{2,1,0:T(8,128)(2,1)}), bf16[4,64,2560]{2,1,0:T(8,128)(2,1)S(1)}, u32[]{:S(2)}, u32[]{:S(2)}) %all-to-all-start) | async-done | bytes 1310752 | tf_op jit(solution)/shard_map/all_to_all | solution.py:46
  44.1 93.8 %all-gather.2.cloned.1.call-done = bf16[4096,896]{1,0:T(8,128)(2,1)} async-done(((bf16[256,896]{1,0:T(8,128)(2,1)}), bf16[4096,896]{1,0:T(8,128)(2,1)}) %all-gather.2.cloned.1.call-update) | async-done | bytes 7340048 | tf_op jit(solution)/shard_map/all_gather | solution.py:75
  137.9 2.6 %collective-permute-start.1 = (bf16[4096,896]{1,0:T(8,128)(2,1)}, bf16[4096,896]{1,0:T(8,128)(2,1)}, u32[]{:S(2)}, u32[]{:S(2)}) collective-permute-start(bf16[4096,896]{1,0:T(8,128)(2,1)} %all-gather.2.cloned.1.call-done), channel_id=1, source_target_pairs={{0,4},{4,0},{1,5},{5,1},{2,6},{6,2},{3,7},{7,3},{8,12},{12,8},{9,1... | collective-permute-start | bytes 22020104 | tf_op jit(solution)/shard_map/ppermute | solution.py:76
  140.5 0.7 slice.123
  141.2 0.8 dynamic_slice.6
  142.2 1.9 collective-permute-start
  144.1 0.6 slice.180
  144.7 0.6 slice.178
  145.3 0.6 convert_reduce_fusion.4
  146.5 0.6 select_reduce_fusion
  147.1 2.5 %broadcast_compare_fusion = (pred[256]{0:T(512)(128)(4,1)S(1)}, f32[256]{0:T(256)}, pred[256]{0:T(512)(128)(4,1)S(1)}) fusion(s32[256]{0:T(256)S(1)} %compare_select_fusion.3, s32[]{:T(128)} %bitcast.18, s32[]{:T(128)} %bitcast.29, pred[]{:T(512)} %gt.8, s32[]{:T(128)} %select_reduce_fusion), kind=kLoop, calls=%fused_computation.132 | loop fusion | flops 1280 | bytes 2573 | tf_op jit(solution)/shard_map/eq | solution.py:169
  149.7 0.1 fusion.16
  152.4 0.3 maximum_maximum_fusion
  152.7 2.4 %copy.131 = bf16[264,2560]{0,1:T(8,128)(2,1)} copy(bf16[264,2560]{1,0:T(8,128)(2,1)S(1)} %maximum_maximum_fusion) | data formatting | bytes 2703360 | tf_op jit(solution)/shard_map/concatenate | solution.py:91
  155.1 2.5 %reshape.411 = bf16[264,4,16,2,20]{0,4,3,2,1:T(8,128)(2,1)S(1)} reshape(bf16[264,2560]{0,1:T(8,128)(2,1)} %copy.131) | data formatting | bytes 2703360 | tf_op jit(solution)/shard_map/reshape | solution.py:84
  157.7 0.6 pad_bitcast_fusion
  158.3 0.4 copy.132
  158.7 6.5 %fusion.65 = f32[264,896]{0,1:T(8,128)S(1)} fusion(bf16[264,4096]{0,1:T(8,128)(2,1)S(1)} %bitcast.140, bf16[4096,896]{1,0:T(8,128)(2,1)} %collective-permute-done.1), kind=kOutput, calls=%fused_computation.137 | convolution fusion | flops 1937768448 | bytes 10448896 | tf_op jit(solution)/shard_map/dot_general | solution.py:96
  165.3 4.0 %select_convert_fusion = (bf16[264,896]{0,1:T(8,128)(2,1)S(1)}, f32[264,896]{0,1:T(8,128)S(1)}) fusion(f32[264,896]{0,1:T(8,128)S(1)} %fusion.65, pred[]{:T(512)S(6)} %eq.70, bf16[264,4096]{0,1:T(8,128)(2,1)S(1)} %bitcast.141, bf16[4096,896]{1,0:T(8,128)(2,1)S(1)} %bitcast.162), kind=kOutput, calls=%fused_computation.2 | convolution fusion | flops 1938004992 | bytes 11868161 | tf_op jit(solution)/shard_map/dot_general | solution.py:95
  169.3 0.1 broadcast_select_fusion
  169.5 0.5 copy-done.2
  170.0 0.7 multiply_bitcast_fusion.1
  170.7 0.6 reduce-window.19
  171.3 0.2 slice_reduce_fusion
  171.5 0.1 copy.139
  171.6 0.2 multiply_reduce_fusion.1
  172.0 0.2 slice_reduce_fusion.1
  172.2 0.1 fusion.49
  172.3 1.5 multiply_convert_fusion.4
  173.8 0.1 fusion.12
  173.9 0.2 convolution_convert_fusion
  174.3 0.7 pad_maximum_fusion.1
  175.0 3.3 %collective-permute-start.3 = (bf16[10,72,128]{2,1,0:T(8,128)(2,1)}, bf16[10,72,128]{2,1,0:T(8,128)(2,1)}, u32[]{:S(2)}, u32[]{:S(2)}) collective-permute-start(bf16[10,72,128]{2,1,0:T(8,128)(2,1)} %pad_maximum_fusion.1), channel_id=1, source_target_pairs={{0,8},{4,12},{8,16},{12,20},{16,24},{20,28},{24,32},{28,36},{32,40... | collective-permute-start | bytes 552968 | tf_op jit(solution)/shard_map/ppermute | solution.py:14
  178.2 2.0 collective-permute-start.2
  180.3 4.9 %collective-permute-start.4 = (bf16[10,72,128]{2,1,0:T(8,128)(2,1)}, bf16[10,72,128]{2,1,0:T(8,128)(2,1)}, u32[]{:S(2)}, u32[]{:S(2)}) collective-permute-start(bf16[10,72,128]{2,1,0:T(8,128)(2,1)} %pad_maximum_fusion.1), channel_id=1, source_target_pairs={{0,12},{4,16},{8,20},{12,24},{16,28},{20,32},{24,36},{28,40},{32,4... | collective-permute-start | bytes 552968 | tf_op jit(solution)/shard_map/ppermute | solution.py:14
  185.2 0.9 fusion.43
  186.2 0.7 exponential_multiply_fusion
  186.9 0.9 copy.146
  187.8 4.0 %all-to-all-start.3 = ((bf16[4,64,640]{2,1,0:T(8,128)(2,1)}), bf16[4,64,640]{2,1,0:T(8,128)(2,1)S(1)}, u32[]{:S(2)}, u32[]{:S(2)}) async-start(bf16[4,64,640]{2,1,0:T(8,128)(2,1)} %bitcast.36), calls=%async_computation.3 | async-start | bytes 655360 | tf_op jit(solution)/shard_map/all_to_all | solution.py:107
  191.8 1.9 fusion.7
  193.8 0.9 fusion.51
  194.7 0.9 fusion.52
  195.5 1.4 fusion.11
  196.9 0.3 convert_element_type.179
  197.2 1.4 copy.144
  198.6 2.0 add_bitcast_fusion
  200.7 4.2 %all-to-all-start.2 = ((bf16[4,64,640]{2,1,0:T(8,128)(2,1)}), bf16[4,64,640]{2,1,0:T(8,128)(2,1)S(1)}, u32[]{:S(2)}, u32[]{:S(2)}) async-start(bf16[4,64,640]{2,1,0:T(8,128)(2,1)} %copy.144), calls=%async_computation.2 | async-start | bytes 655360 | tf_op jit(solution)/shard_map/all_to_all | solution.py:227
  205.0 0.4 copy.147
  205.4 6.0 %all-to-all-done.2 = bf16[4,64,640]{2,1,0:T(8,128)(2,1)S(1)} async-done(((bf16[4,64,640]{2,1,0:T(8,128)(2,1)}), bf16[4,64,640]{2,1,0:T(8,128)(2,1)S(1)}, u32[]{:S(2)}, u32[]{:S(2)}) %all-to-all-start.2) | async-done | bytes 327712 | tf_op jit(solution)/shard_map/all_to_all | solution.py:227
  211.4 0.3 multiply_reduce_fusion
  211.8 0.4 copy.145
  212.3 1.0 multiply_convert_fusion.5
  (71 shorter events, 1.1 us)
Async XLA Ops:
  9.4 11.3 %all-to-all-start.1 = ((bf16[2,32,896]{2,1,0:T(8,128)(2,1)}), bf16[2,32,896]{2,1,0:T(8,128)(2,1)S(1)}, u32[]{:S(2)}, u32[]{:S(2)}) async-start(bf16[2,32,896]{2,1,0:T(8,128)(2,1)} %pad_maximum_fusion.2), calls=%async_computation.1 | async-start | bytes 229376 | tf_op jit(solution)/shard_map/all_to_all | solution.py:58
  20.7 121.3 %copy-start = (f32[4,2816]{1,0:T(4,128)S(1)}, f32[4,2816]{1,0:T(4,128)}, u32[]{:S(2)}) copy-start(f32[4,2816]{1,0:T(4,128)} %param.17) | copy-start | bytes 135172
  20.8 121.3 %slice-start = ((f32[4,2816]{1,0:T(4,128)}), f32[4,256]{1,0:T(4,128)S(1)}, s32[]{:S(2)}) async-start(f32[4,2816]{1,0:T(4,128)} %param.17), calls=%async_computation.5 | async-start | bytes 8192 | tf_op jit(solution)/shard_map/slice | solution.py:113
  22.9 21.2 %all-to-all-start = ((bf16[4,64,2560]{2,1,0:T(8,128)(2,1)}), bf16[4,64,2560]{2,1,0:T(8,128)(2,1)S(1)}, u32[]{:S(2)}, u32[]{:S(2)}) async-start(bf16[4,64,2560]{2,1,0:T(8,128)(2,1)} %broadcast_in_dim.39), calls=%async_computation | async-start | bytes 2621440 | tf_op jit(solution)/shard_map/all_to_all | solution.py:46
  26.5 111.5 %all-gather.2.cloned.1.call-start = ((), (), s32[]{:S(2)}) async-start(), calls=%async_computation.4 | async-start | bytes 7798784 | tf_op jit(solution)/shard_map/all_gather | solution.py:75
  137.9 20.8 %collective-permute-start.1 = (bf16[4096,896]{1,0:T(8,128)(2,1)}, bf16[4096,896]{1,0:T(8,128)(2,1)}, u32[]{:S(2)}, u32[]{:S(2)}) collective-permute-start(bf16[4096,896]{1,0:T(8,128)(2,1)} %all-gather.2.cloned.1.call-done), channel_id=1, source_target_pairs={{0,4},{4,0},{1,5},{5,1},{2,6},{6,2},{3,7},{7,3},{8,12},{12,8},{9,1... | collective-permute-start | bytes 22020104 | tf_op jit(solution)/shard_map/ppermute | solution.py:76
  142.2 10.2 %collective-permute-start = (bf16[3,2560]{1,0:T(4,128)(2,1)S(1)}, bf16[3,2560]{1,0:T(4,128)(2,1)S(1)}, u32[]{:S(2)}, u32[]{:S(2)}) collective-permute-start(bf16[3,2560]{1,0:T(4,128)(2,1)S(1)} %slice.128), channel_id=1, source_target_pairs={{0,4},{4,8},{8,12},{12,16},{16,20},{20,24},{24,28},{28,32},{32,36}... | collective-permute-start | bytes 46088 | tf_op jit(solution)/shard_map/ppermute | solution.py:14
  158.3 7.0 %slice-start.1 = ((s8[7340032]{0:T(1024)(128)(4,1)}), s8[4194304]{0:T(1024)(128)(4,1)S(1)}, s32[]{:S(2)}) async-start(s8[7340032]{0:T(1024)(128)(4,1)} %bitcast.161), calls=%async_computation.6 | async-start | bytes 8388608
  158.7 6.5 %slice-start.2 = ((s8[7340032]{0:T(1024)(128)(4,1)}), s8[3145728]{0:T(1024)(128)(4,1)S(1)}, s32[]{:S(2)}) async-start(s8[7340032]{0:T(1024)(128)(4,1)} %bitcast.161), calls=%async_computation.7 | async-start | bytes 6291456
  169.3 0.7 copy-start.2
  169.3 0.7 copy-start.5
  171.8 13.4 %copy-start.4 = (f32[10]{0:T(128)}, f32[10]{0:T(128)S(1)}, u32[]{:S(2)}) copy-start(f32[10]{0:T(128)S(1)} %multiply_reduce_fusion.1) | copy-start | bytes 124
  175.0 18.8 %collective-permute-start.3 = (bf16[10,72,128]{2,1,0:T(8,128)(2,1)}, bf16[10,72,128]{2,1,0:T(8,128)(2,1)}, u32[]{:S(2)}, u32[]{:S(2)}) collective-permute-start(bf16[10,72,128]{2,1,0:T(8,128)(2,1)} %pad_maximum_fusion.1), channel_id=1, source_target_pairs={{0,8},{4,12},{8,16},{12,20},{16,24},{20,28},{24,32},{28,36},{32,40... | collective-permute-start | bytes 552968 | tf_op jit(solution)/shard_map/ppermute | solution.py:14
  178.2 16.4 %collective-permute-start.2 = (bf16[10,72,128]{2,1,0:T(8,128)(2,1)}, bf16[10,72,128]{2,1,0:T(8,128)(2,1)}, u32[]{:S(2)}, u32[]{:S(2)}) collective-permute-start(bf16[10,72,128]{2,1,0:T(8,128)(2,1)} %pad_maximum_fusion.1), channel_id=1, source_target_pairs={{0,4},{4,8},{8,12},{12,16},{16,20},{20,24},{24,28},{28,32},{32,36}... | collective-permute-start | bytes 552968 | tf_op jit(solution)/shard_map/ppermute | solution.py:14
  180.3 15.3 %collective-permute-start.4 = (bf16[10,72,128]{2,1,0:T(8,128)(2,1)}, bf16[10,72,128]{2,1,0:T(8,128)(2,1)}, u32[]{:S(2)}, u32[]{:S(2)}) collective-permute-start(bf16[10,72,128]{2,1,0:T(8,128)(2,1)} %pad_maximum_fusion.1), channel_id=1, source_target_pairs={{0,12},{4,16},{8,20},{12,24},{16,28},{20,32},{24,36},{28,40},{32,4... | collective-permute-start | bytes 552968 | tf_op jit(solution)/shard_map/ppermute | solution.py:14
  187.8 12.9 %all-to-all-start.3 = ((bf16[4,64,640]{2,1,0:T(8,128)(2,1)}), bf16[4,64,640]{2,1,0:T(8,128)(2,1)S(1)}, u32[]{:S(2)}, u32[]{:S(2)}) async-start(bf16[4,64,640]{2,1,0:T(8,128)(2,1)} %bitcast.36), calls=%async_computation.3 | async-start | bytes 655360 | tf_op jit(solution)/shard_map/all_to_all | solution.py:107
  191.8 1.9 copy-start.3
  191.8 3.7 %copy-start.6 = (f32[10]{0:T(128)S(1)}, f32[10]{0:T(128)}, u32[]{:S(2)}) copy-start(f32[10]{0:T(128)} %param.21) | copy-start | bytes 124
  200.7 10.8 %all-to-all-start.2 = ((bf16[4,64,640]{2,1,0:T(8,128)(2,1)}), bf16[4,64,640]{2,1,0:T(8,128)(2,1)S(1)}, u32[]{:S(2)}, u32[]{:S(2)}) async-start(bf16[4,64,640]{2,1,0:T(8,128)(2,1)} %copy.144), calls=%async_computation.2 | async-start | bytes 655360 | tf_op jit(solution)/shard_map/all_to_all | solution.py:227
  205.4 6.9 %copy-start.1 = (f32[2560]{0:T(1024)S(1)}, f32[2560]{0:T(1024)}, u32[]{:S(2)}) copy-start(f32[2560]{0:T(1024)} %param.22) | copy-start | bytes 30724
Sparse Core Ops, SparseCore 0:
  44.2 93.6 all-gather.1
where the time goes:
time: 221 us; the launch traced here: 220 us
  waiting for transfers between devices  106 us (48%)
  starting transfers between devices  36.7 us (17%)
  between operations  17.7 us (8%)
  local copies, waits for them, and re-layouts  17.1 us (8%)
  matrix products  17 us (8%)
  other arithmetic  14.2 us (6%)
  blocking collectives  11.1 us (5%)
    all_gather x1, waiting for transfers between devices, on_device(): own_half = lax.all_gather(own_half, 'z', axis=0, tiled=True)  93.8 us
    ppermute x4, starting transfers between devices, from_behind(): return lax.ppermute(block, axis, route)  12.1 us
    all_gather x1, blocking collectives, on_device(): own_half = lax.all_gather(own_half, 'x', axis=0, tiled=True)  11.1 us
    all_to_all x1, starting transfers between devices, on_device(): lax.all_to_all(halves, 'c', 0, 0, tiled=True).reshape(2 * padded_rows, half)  10.2 us
    dot_general x1, matrix products, on_device(): with_other = jnp.dot(spread, other_half, preferred_element_type=jnp.float32)  6.52 us
    all_to_all x1, waiting for transfers between devices, on_device(): lax.all_to_all(jnp.broadcast_to(hidden[None], (groups,) + hidden.shape),...  6.39 us
    all_to_all x1, waiting for transfers between devices, on_device(): lax.all_to_all(ssm_rows.reshape(groups, sub_rows, local_width), 'head', 0...  5.98 us
  transfers between devices with their start and end apart: 10, of which 3 were waited for; matrix products, arithmetic and copies ran while one was open for 12% of the time, Pallas kernels for 0%

commit v1 on v0

--- a/solution.py
+++ b/solution.py
@@ -2,6 +2,7 @@
 import jax.numpy as jnp
 from jax import lax
 from jax.sharding import Mesh, PartitionSpec as P
+from jax.lax import all_to_all, psum
 
 STRETCH = 256
 SEQ = ("x", "z", "c")
@@ -33,6 +34,18 @@
     norm_gain,
     lengths,
 ):
+
+    def test_the_blocks(shard_in, comm_axis):
+        return jnp.concatenate(
+            all_to_all(
+                jnp.stack(jnp.split(shard_in, psum(1, comm_axis), 0), 0),
+                comm_axis,
+                split_axis=0,
+                concat_axis=0,
+            ),
+            2,
+        )
+
     groups = lax.axis_size("head")
     group_index = lax.axis_index("head")
     block_index = lax.axis_index(SEQ)
@@ -224,9 +237,9 @@
     )
     end_states = end_states + end_carry[:, :, None, None] * arriving
     final_block = jnp.sum(end_states, axis=0)[None]
-    y_tokens = lax.all_to_all(
-        ssm_rows.reshape(groups, sub_rows, local_width), "head", 0, 2, tiled=True
-    ).reshape(sub_rows, inner_width)
+    y_tokens = test_the_blocks(ssm_rows.reshape(groups, sub_rows, local_width), "head").reshape(
+        sub_rows, inner_width
+    )
     token_rows = (y_tokens.astype(jnp.float32), gates_tokens.astype(jnp.float32))
     gated = token_rows[0] * jax.nn.silu(token_rows[1])
     mean_square = jnp.mean(gated * gated, axis=1)

time: 221 us -> 221 us (level)
  no operation moved by 1% of the time
where the time goes in v1:
time: 221 us; the launch traced here: 220 us
  waiting for transfers between devices  106 us (48%)
  starting transfers between devices  36.7 us (17%)
  between operations  17.7 us (8%)
  matrix products  17 us (8%)
  local copies, waits for them, and re-layouts  16.2 us (7%)
  other arithmetic  15 us (7%)
  blocking collectives  11.1 us (5%)
    all_gather x1, waiting for transfers between devices, on_device(): own_half = lax.all_gather(own_half, 'z', axis=0, tiled=True)  93.8 us
    ppermute x4, starting transfers between devices, from_behind(): return lax.ppermute(block, axis, route)  12.1 us
    all_gather x1, blocking collectives, on_device(): own_half = lax.all_gather(own_half, 'x', axis=0, tiled=True)  11.1 us
    all_to_all x1, starting transfers between devices, on_device(): lax.all_to_all(halves, 'c', 0, 0, tiled=True).reshape(2 * padded_rows, half)  10.2 us
    dot_general x1, matrix products, on_device(): with_other = jnp.dot(spread, other_half, preferred_element_type=jnp.float32)  6.52 us
    all_to_all x1, waiting for transfers between devices, on_device(): lax.all_to_all(jnp.broadcast_to(hidden[None], (groups,) + hidden.shape),...  6.39 us
    all_to_all x1, waiting for transfers between devices, test_the_blocks(): all_to_all(jnp.stack(jnp.split(shard_in, psum(1, comm_axis), 0), 0), comm...  5.99 us
  transfers between devices with their start and end apart: 10, of which 3 were waited for; matrix products, arithmetic and copies ran while one was open for 12% of the time, Pallas kernels for 0%

profile of v1, /device:TPU:1, one launch (start us, length us, event | category | flops | bytes accessed | tf_op | source)
XLA Modules:
  0.0 220.0 jit_solution(18335017534258997284)
XLA Ops:
  7.2 0.8 copy.171
  8.0 0.8 fusion.32
  8.8 0.7 pad_maximum_fusion.3
  9.4 10.2 %all-to-all-start.1 = ((bf16[2,32,896]{2,1,0:T(8,128)(2,1)}), bf16[2,32,896]{2,1,0:T(8,128)(2,1)S(1)}, u32[]{:S(2)}, u32[]{:S(2)}) async-start(bf16[2,32,896]{2,1,0:T(8,128)(2,1)} %pad_maximum_fusion.3), calls=%async_computation.1 | async-start | bytes 229376 | tf_op jit(solution)/shard_map/all_to_all | solution.py:71
  19.7 0.7 copy.172
  20.5 0.1 reduce.8
  20.8 2.1 broadcast_in_dim.39
  22.9 3.5 %all-to-all-start = ((bf16[4,64,2560]{2,1,0:T(8,128)(2,1)}), bf16[4,64,2560]{2,1,0:T(8,128)(2,1)S(1)}, u32[]{:S(2)}, u32[]{:S(2)}) async-start(bf16[4,64,2560]{2,1,0:T(8,128)(2,1)} %broadcast_in_dim.39), calls=%async_computation | async-start | bytes 2621440 | tf_op jit(solution)/shard_map/all_to_all | solution.py:59
  26.5 0.1 convert_reduce_fusion.1
  26.6 11.1 %all_gather.6 = bf16[256,896]{1,0:T(8,128)(2,1)} all-gather(bf16[64,896]{1,0:T(8,128)(2,1)S(1)} %bitcast.151), channel_id=1, replica_groups=mesh['x'=4,'z'=16,'c'=2,'head'=4] {'x'}, dimensions={0}, use_global_device_ids=true | all-gather | bytes 573440 | tf_op jit(solution)/shard_map/all_gather | solution.py:72
  37.7 6.4 %all-to-all-done = bf16[4,64,2560]{2,1,0:T(8,128)(2,1)S(1)} async-done(((bf16[4,64,2560]{2,1,0:T(8,128)(2,1)}), bf16[4,64,2560]{2,1,0:T(8,128)(2,1)S(1)}, u32[]{:S(2)}, u32[]{:S(2)}) %all-to-all-start) | async-done | bytes 1310752 | tf_op jit(solution)/shard_map/all_to_all | solution.py:59
  44.1 93.8 %all-gather.2.cloned.1.call-done = bf16[4096,896]{1,0:T(8,128)(2,1)} async-done(((bf16[256,896]{1,0:T(8,128)(2,1)}), bf16[4096,896]{1,0:T(8,128)(2,1)}) %all-gather.2.cloned.1.call-update) | async-done | bytes 7340048 | tf_op jit(solution)/shard_map/all_gather | solution.py:88
  137.9 2.6 %collective-permute-start.1 = (bf16[4096,896]{1,0:T(8,128)(2,1)}, bf16[4096,896]{1,0:T(8,128)(2,1)}, u32[]{:S(2)}, u32[]{:S(2)}) collective-permute-start(bf16[4096,896]{1,0:T(8,128)(2,1)} %all-gather.2.cloned.1.call-done), channel_id=1, source_target_pairs={{0,4},{4,0},{1,5},{5,1},{2,6},{6,2},{3,7},{7,3},{8,12},{12,8},{9,1... | collective-permute-start | bytes 22020104 | tf_op jit(solution)/shard_map/ppermute | solution.py:89
  140.5 0.7 slice.131
  141.2 0.8 dynamic_slice.6
  142.2 1.9 collective-permute-start
  144.1 0.6 slice.188
  144.7 0.6 slice.186
  145.3 0.6 convert_reduce_fusion.4
  146.5 0.6 select_reduce_fusion
  147.1 2.5 %broadcast_compare_fusion = (pred[256]{0:T(512)(128)(4,1)S(1)}, f32[256]{0:T(256)}, pred[256]{0:T(512)(128)(4,1)S(1)}) fusion(s32[256]{0:T(256)S(1)} %compare_select_fusion.3, s32[]{:T(128)} %bitcast.18, s32[]{:T(128)} %bitcast.29, pred[]{:T(512)} %gt.8, s32[]{:T(128)} %select_reduce_fusion), kind=kLoop, calls=%fused_computation.133 | loop fusion | flops 1280 | bytes 2573 | tf_op jit(solution)/shard_map/eq | solution.py:182
  149.7 0.1 fusion.16
  152.4 0.3 maximum_maximum_fusion
  152.7 2.4 %copy.173 = bf16[264,2560]{0,1:T(8,128)(2,1)} copy(bf16[264,2560]{1,0:T(8,128)(2,1)S(1)} %maximum_maximum_fusion) | data formatting | bytes 2703360 | tf_op jit(solution)/shard_map/concatenate | solution.py:104
  155.1 2.5 %reshape.421 = bf16[264,4,16,2,20]{0,4,3,2,1:T(8,128)(2,1)S(1)} reshape(bf16[264,2560]{0,1:T(8,128)(2,1)} %copy.173) | data formatting | bytes 2703360 | tf_op jit(solution)/shard_map/reshape | solution.py:97
  157.7 0.6 pad_bitcast_fusion
  158.3 0.4 copy.174
  158.7 6.5 %fusion.66 = f32[264,896]{0,1:T(8,128)S(1)} fusion(bf16[264,4096]{0,1:T(8,128)(2,1)S(1)} %bitcast.139, bf16[4096,896]{1,0:T(8,128)(2,1)} %collective-permute-done.1), kind=kOutput, calls=%fused_computation.139 | convolution fusion | flops 1937768448 | bytes 10448896 | tf_op jit(solution)/shard_map/dot_general | solution.py:109
  165.3 4.0 %select_convert_fusion = (bf16[264,896]{0,1:T(8,128)(2,1)S(1)}, f32[264,896]{0,1:T(8,128)S(1)}) fusion(f32[264,896]{0,1:T(8,128)S(1)} %fusion.66, pred[]{:T(512)S(6)} %eq.70, bf16[264,4096]{0,1:T(8,128)(2,1)S(1)} %bitcast.140, bf16[4096,896]{1,0:T(8,128)(2,1)S(1)} %bitcast.165), kind=kOutput, calls=%fused_computation.2 | convolution fusion | flops 1938004992 | bytes 11868161 | tf_op jit(solution)/shard_map/dot_general | solution.py:108
  169.3 0.1 broadcast_select_fusion
  169.5 0.5 copy-done.2
  170.0 0.7 multiply_bitcast_fusion.1
  170.7 0.6 reduce-window.19
  171.3 0.2 slice_reduce_fusion
  171.6 0.2 multiply_reduce_fusion.1
  172.0 0.2 slice_reduce_fusion.1
  172.3 1.5 multiply_convert_fusion.4
  173.8 0.1 fusion.12
  173.9 0.2 convolution_convert_fusion
  174.3 0.7 pad_maximum_fusion.2
  175.0 3.3 %collective-permute-start.3 = (bf16[10,72,128]{2,1,0:T(8,128)(2,1)}, bf16[10,72,128]{2,1,0:T(8,128)(2,1)}, u32[]{:S(2)}, u32[]{:S(2)}) collective-permute-start(bf16[10,72,128]{2,1,0:T(8,128)(2,1)} %pad_maximum_fusion.2), channel_id=1, source_target_pairs={{0,8},{4,12},{8,16},{12,20},{16,24},{20,28},{24,32},{28,36},{32,40... | collective-permute-start | bytes 552968 | tf_op jit(solution)/shard_map/ppermute | solution.py:15
  178.2 2.0 collective-permute-start.2
  180.3 4.9 %collective-permute-start.4 = (bf16[10,72,128]{2,1,0:T(8,128)(2,1)}, bf16[10,72,128]{2,1,0:T(8,128)(2,1)}, u32[]{:S(2)}, u32[]{:S(2)}) collective-permute-start(bf16[10,72,128]{2,1,0:T(8,128)(2,1)} %pad_maximum_fusion.2), channel_id=1, source_target_pairs={{0,12},{4,16},{8,20},{12,24},{16,28},{20,32},{24,36},{28,40},{32,4... | collective-permute-start | bytes 552968 | tf_op jit(solution)/shard_map/ppermute | solution.py:15
  185.2 0.9 fusion.43
  186.2 0.7 exponential_multiply_fusion
  186.9 0.9 copy.192
  187.8 4.0 %all-to-all-start.3 = ((bf16[4,64,640]{2,1,0:T(8,128)(2,1)}), bf16[4,64,640]{2,1,0:T(8,128)(2,1)S(1)}, u32[]{:S(2)}, u32[]{:S(2)}) async-start(bf16[4,64,640]{2,1,0:T(8,128)(2,1)} %bitcast.40), calls=%async_computation.3 | async-start | bytes 655360 | tf_op jit(solution)/shard_map/all_to_all | solution.py:120
  191.8 1.9 fusion.7
  193.8 0.9 fusion.51
  194.7 0.9 fusion.52
  195.5 1.4 fusion.11
  196.9 0.2 fusion.65
  197.1 0.1 copy.186
  197.3 0.1 copy.187
  197.4 0.1 copy.188
  197.6 0.1 copy.189
  197.7 0.8 pad_maximum_fusion.1
  198.5 2.0 add_bitcast_fusion
  200.6 4.2 %all-to-all-start.2 = ((bf16[4,1,64,640]{3,2,1,0:T(8,128)(2,1)}), bf16[4,1,64,640]{3,2,1,0:T(8,128)(2,1)S(1)}, u32[]{:S(2)}, u32[]{:S(2)}) async-start(bf16[4,1,64,640]{3,2,1,0:T(8,128)(2,1)} %pad_maximum_fusion.1), calls=%async_computation.2 | async-start | bytes 655360 | tf_op jit(solution)/shard_map/all_to_all | solution.py:40
  204.8 0.4 copy.193
  205.3 6.0 %all-to-all-done.2 = bf16[4,1,64,640]{3,2,1,0:T(8,128)(2,1)S(1)} async-done(((bf16[4,1,64,640]{3,2,1,0:T(8,128)(2,1)}), bf16[4,1,64,640]{3,2,1,0:T(8,128)(2,1)S(1)}, u32[]{:S(2)}, u32[]{:S(2)}) %all-to-all-start.2) | async-done | bytes 327712 | tf_op jit(solution)/shard_map/all_to_all | solution.py:40
  211.3 0.3 multiply_reduce_fusion
  211.7 0.4 copy.191
  212.2 1.0 multiply_convert_fusion.5
  (75 shorter events, 1.5 us)
Async XLA Ops:
  9.4 11.3 %all-to-all-start.1 = ((bf16[2,32,896]{2,1,0:T(8,128)(2,1)}), bf16[2,32,896]{2,1,0:T(8,128)(2,1)S(1)}, u32[]{:S(2)}, u32[]{:S(2)}) async-start(bf16[2,32,896]{2,1,0:T(8,128)(2,1)} %pad_maximum_fusion.3), calls=%async_computation.1 | async-start | bytes 229376 | tf_op jit(solution)/shard_map/all_to_all | solution.py:71
  20.7 121.3 %copy-start = (f32[4,2816]{1,0:T(4,128)S(1)}, f32[4,2816]{1,0:T(4,128)}, u32[]{:S(2)}) copy-start(f32[4,2816]{1,0:T(4,128)} %param.17) | copy-start | bytes 135172
  20.8 121.3 %slice-start = ((f32[4,2816]{1,0:T(4,128)}), f32[4,256]{1,0:T(4,128)S(1)}, s32[]{:S(2)}) async-start(f32[4,2816]{1,0:T(4,128)} %param.17), calls=%async_computation.5 | async-start | bytes 8192 | tf_op jit(solution)/shard_map/slice | solution.py:126
  22.9 21.2 %all-to-all-start = ((bf16[4,64,2560]{2,1,0:T(8,128)(2,1)}), bf16[4,64,2560]{2,1,0:T(8,128)(2,1)S(1)}, u32[]{:S(2)}, u32[]{:S(2)}) async-start(bf16[4,64,2560]{2,1,0:T(8,128)(2,1)} %broadcast_in_dim.39), calls=%async_computation | async-start | bytes 2621440 | tf_op jit(solution)/shard_map/all_to_all | solution.py:59
  26.5 111.5 %all-gather.2.cloned.1.call-start = ((), (), s32[]{:S(2)}) async-start(), calls=%async_computation.4 | async-start | bytes 7798784 | tf_op jit(solution)/shard_map/all_gather | solution.py:88
  137.9 20.8 %collective-permute-start.1 = (bf16[4096,896]{1,0:T(8,128)(2,1)}, bf16[4096,896]{1,0:T(8,128)(2,1)}, u32[]{:S(2)}, u32[]{:S(2)}) collective-permute-start(bf16[4096,896]{1,0:T(8,128)(2,1)} %all-gather.2.cloned.1.call-done), channel_id=1, source_target_pairs={{0,4},{4,0},{1,5},{5,1},{2,6},{6,2},{3,7},{7,3},{8,12},{12,8},{9,1... | collective-permute-start | bytes 22020104 | tf_op jit(solution)/shard_map/ppermute | solution.py:89
  142.2 10.2 %collective-permute-start = (bf16[3,2560]{1,0:T(4,128)(2,1)S(1)}, bf16[3,2560]{1,0:T(4,128)(2,1)S(1)}, u32[]{:S(2)}, u32[]{:S(2)}) collective-permute-start(bf16[3,2560]{1,0:T(4,128)(2,1)S(1)} %slice.136), channel_id=1, source_target_pairs={{0,4},{4,8},{8,12},{12,16},{16,20},{20,24},{24,28},{28,32},{32,36}... | collective-permute-start | bytes 46088 | tf_op jit(solution)/shard_map/ppermute | solution.py:15
  158.3 7.0 %slice-start.1 = ((s8[7340032]{0:T(1024)(128)(4,1)}), s8[4194304]{0:T(1024)(128)(4,1)S(1)}, s32[]{:S(2)}) async-start(s8[7340032]{0:T(1024)(128)(4,1)} %bitcast.164), calls=%async_computation.6 | async-start | bytes 8388608
  158.7 6.5 %slice-start.2 = ((s8[7340032]{0:T(1024)(128)(4,1)}), s8[3145728]{0:T(1024)(128)(4,1)S(1)}, s32[]{:S(2)}) async-start(s8[7340032]{0:T(1024)(128)(4,1)} %bitcast.164), calls=%async_computation.7 | async-start | bytes 6291456
  169.3 0.7 copy-start.2
  169.3 0.7 copy-start.5
  171.8 13.4 %copy-start.4 = (f32[10]{0:T(128)}, f32[10]{0:T(128)S(1)}, u32[]{:S(2)}) copy-start(f32[10]{0:T(128)S(1)} %multiply_reduce_fusion.1) | copy-start | bytes 124
  175.0 18.8 %collective-permute-start.3 = (bf16[10,72,128]{2,1,0:T(8,128)(2,1)}, bf16[10,72,128]{2,1,0:T(8,128)(2,1)}, u32[]{:S(2)}, u32[]{:S(2)}) collective-permute-start(bf16[10,72,128]{2,1,0:T(8,128)(2,1)} %pad_maximum_fusion.2), channel_id=1, source_target_pairs={{0,8},{4,12},{8,16},{12,20},{16,24},{20,28},{24,32},{28,36},{32,40... | collective-permute-start | bytes 552968 | tf_op jit(solution)/shard_map/ppermute | solution.py:15
  178.2 16.4 %collective-permute-start.2 = (bf16[10,72,128]{2,1,0:T(8,128)(2,1)}, bf16[10,72,128]{2,1,0:T(8,128)(2,1)}, u32[]{:S(2)}, u32[]{:S(2)}) collective-permute-start(bf16[10,72,128]{2,1,0:T(8,128)(2,1)} %pad_maximum_fusion.2), channel_id=1, source_target_pairs={{0,4},{4,8},{8,12},{12,16},{16,20},{20,24},{24,28},{28,32},{32,36}... | collective-permute-start | bytes 552968 | tf_op jit(solution)/shard_map/ppermute | solution.py:15
  180.3 15.3 %collective-permute-start.4 = (bf16[10,72,128]{2,1,0:T(8,128)(2,1)}, bf16[10,72,128]{2,1,0:T(8,128)(2,1)}, u32[]{:S(2)}, u32[]{:S(2)}) collective-permute-start(bf16[10,72,128]{2,1,0:T(8,128)(2,1)} %pad_maximum_fusion.2), channel_id=1, source_target_pairs={{0,12},{4,16},{8,20},{12,24},{16,28},{20,32},{24,36},{28,40},{32,4... | collective-permute-start | bytes 552968 | tf_op jit(solution)/shard_map/ppermute | solution.py:15
  187.8 12.7 %all-to-all-start.3 = ((bf16[4,64,640]{2,1,0:T(8,128)(2,1)}), bf16[4,64,640]{2,1,0:T(8,128)(2,1)S(1)}, u32[]{:S(2)}, u32[]{:S(2)}) async-start(bf16[4,64,640]{2,1,0:T(8,128)(2,1)} %bitcast.40), calls=%async_computation.3 | async-start | bytes 655360 | tf_op jit(solution)/shard_map/all_to_all | solution.py:120
  191.8 1.9 copy-start.3
  191.8 3.7 %copy-start.6 = (f32[10]{0:T(128)S(1)}, f32[10]{0:T(128)}, u32[]{:S(2)}) copy-start(f32[10]{0:T(128)} %param.21) | copy-start | bytes 124
  200.6 10.8 %all-to-all-start.2 = ((bf16[4,1,64,640]{3,2,1,0:T(8,128)(2,1)}), bf16[4,1,64,640]{3,2,1,0:T(8,128)(2,1)S(1)}, u32[]{:S(2)}, u32[]{:S(2)}) async-start(bf16[4,1,64,640]{3,2,1,0:T(8,128)(2,1)} %pad_maximum_fusion.1), calls=%async_computation.2 | async-start | bytes 655360 | tf_op jit(solution)/shard_map/all_to_all | solution.py:40
  205.3 6.9 %copy-start.1 = (f32[2560]{0:T(1024)S(1)}, f32[2560]{0:T(1024)}, u32[]{:S(2)}) copy-start(f32[2560]{0:T(1024)} %param.22) | copy-start | bytes 30724
Sparse Core Ops, SparseCore 0:
  44.2 93.6 all-gather.1
